TPU v7x, 512 devices: a whole 4x8x8 slice. The times are simulated.
512 devices in a mesh: section: 16 (over x_hi, y), dp: 8 (over z), mp: 4 (over x_lo, core).
Axes of the slice: x: 4 (x_hi: 2, x_lo: 2; x = x_hi * 2 + x_lo), y: 8, z: 8, core: 2. Of those that a mesh axis runs over, the one named last changes fastest.
Arguments:
- cotangent: bfloat16 [1024, 4096], P('dp', 'mp'), may hold values from -6 to 6
- saved_inputs: bfloat16 [16, 1024, 4096], P('section', 'dp', 'mp'), may hold values from -6 to 6
- pre_acts: bfloat16 [16, 1024, 4096], P('section', 'dp', 'mp'), may hold values from -8 to 8
- weights: bfloat16 [16, 4096, 4096], P('section', 'mp', 'dp'), may hold values from -0.046875 to 0.046875
- proj_in: bfloat16 [16, 4096, 64], P('section', 'mp'), may hold values from -0.09375 to 0.09375
- proj_out: bfloat16 [16, 4096, 64], P('section', 'mp'), may hold values from -0.09375 to 0.09375
- query_panels: float32 [16, 16, 4096], P('section', 'dp', 'mp'), may hold values from -4 to 4
- partners: int32 [8, 8], replicated, may hold values from 0 to 7, as said below
Outputs:
- train_panels: float32 [16, 32, 4096], P('section', 'dp', 'mp')
- scores: float32 [16, 8, 4], replicated
Inputs may be any that keep to these rules, and one draw needn't show every extreme that they name: The plan has 8 rounds: one round pairs every dp index with itself, and the others are the rounds of one round-robin plan of the 8 indices. The rows of partners hold each of these rounds once, in some order, so partners[r, partners[r, i]] = i.
All inputs are finite; a program needn't handle non-finite values.
Results may differ from a plain program's by a relative error of at most 0.02.
Values may be sent and summed in bfloat16 or wider, within the bound.
No kernel may reach another device: no remote copies, remote signals or barrier semaphores. Data moves between devices by JAX's collectives and lax.ppermute only.
A program may use at most 64 MiB of HBM per device.

v0:
```python
import math
import jax
import jax.numpy as jnp
from jax import lax
from jax.sharding import PartitionSpec as P

LEN = 32


def from_behind(block, axis, distance):
    devices = range(lax.axis_size(axis))
    route = [(i - distance, i) for i in devices if i - distance in devices]
    return lax.ppermute(block, axis, route)


def silu_slope(pre_state):
    sigma = jax.nn.sigmoid(pre_state)
    return sigma * (1.0 + pre_state * (1.0 - sigma))


def score_pair(query_rows, train_rows):
    return jnp.dot(query_rows, train_rows.T, precision=lax.Precision.HIGHEST)


def place_block(score_table, block, row_at, col_at):
    return lax.dynamic_update_slice(
        score_table,
        block[None, None],
        (jnp.asarray(row_at, jnp.int32), jnp.int32(col_at), jnp.int32(0), jnp.int32(0)),
    )


def body(cotangent, saved_inputs, pre_acts, weights, proj_in, proj_out, query_panels, partners):
    section_count = lax.axis_size("section")
    model_count = lax.axis_size("mp")
    data_count = lax.axis_size("dp")
    section_index = lax.axis_index("section")
    model_index = lax.axis_index("mp")
    data_index = lax.axis_index("dp")
    inputs = saved_inputs[0]
    pre_state = pre_acts[0]
    columns = inputs.shape[1]
    length = LEN
    examples = inputs.shape[0] // length
    low_rank = proj_in.shape[2]
    w_rows = lax.all_gather(weights[0], "dp", axis=1, tiled=True)
    step_count = examples + section_count - 1
    top_section = section_count - 1

    def advance(turn, carry):
        outgoing, stored, side_store = carry
        received = from_behind(outgoing, "section", -1)
        example_at = turn - (top_section - section_index)
        active = jnp.logical_and(example_at >= 0, example_at < examples)
        row_start = jnp.clip(example_at, 0, examples - 1) * length
        top_grad = lax.dynamic_slice_in_dim(cotangent, row_start, length, 0)
        delta_piece = jnp.where(section_index == top_section, top_grad, received)
        slopes = silu_slope(
            lax.dynamic_slice_in_dim(pre_state, row_start, length, 0).astype(jnp.float32)
        )
        grad_piece = (delta_piece.astype(jnp.float32) * slopes).astype(jnp.bfloat16)
        grad_full = lax.all_gather(grad_piece, "mp", axis=1, tiled=True)

        def through():
            back_term = lax.dot_general(
                grad_full, w_rows, (((1,), (1,)), ((), ())), preferred_element_type=jnp.float32
            )
            return (delta_piece.astype(jnp.float32) + back_term).astype(jnp.bfloat16)

        def skipped():
            return jnp.zeros_like(delta_piece)

        passed = lax.cond(active, through, skipped)
        previous = lax.dynamic_slice_in_dim(stored, row_start, length, 0)
        stored = lax.dynamic_update_slice_in_dim(
            stored, jnp.where(active, grad_piece, previous), row_start, 0
        )
        return (passed, stored, side_store)

    initial = (
        jnp.zeros((length, columns), jnp.bfloat16),
        jnp.zeros((inputs.shape[0], columns), jnp.bfloat16),
        jnp.zeros((inputs.shape[0], low_rank), jnp.float32),
    )
    final_state = lax.fori_loop(0, step_count, advance, initial)
    stored = final_state[1]
    side_store = final_state[2]
    in_part = jnp.dot(inputs, proj_in[0], preferred_element_type=jnp.float32)
    out_part = jnp.dot(stored, proj_out[0], preferred_element_type=jnp.float32)
    in_side, out_side = (
        lax.psum(in_part.astype(jnp.bfloat16), "mp").astype(jnp.float32),
        lax.psum(out_part.astype(jnp.bfloat16), "mp").astype(jnp.float32),
    )
    piece_rank = low_rank // model_count
    in_rows = lax.dynamic_slice_in_dim(in_side, model_index * piece_rank, piece_rank, 1)
    panels_here = jnp.einsum(
        "etr,etc->erc",
        in_rows.reshape(examples, length, piece_rank),
        out_side.reshape(examples, length, low_rank),
        precision=lax.Precision.HIGHEST,
    ) / math.sqrt(length)
    panels_here = panels_here.reshape(examples, piece_rank * low_rank)
    queries = query_panels[0]
    asked = queries.shape[0]
    rounds = partners.shape[0]
    score_scale = 1.0 / (low_rank * math.sqrt(section_count))
    score_table = jnp.zeros((data_count, rounds, asked, examples), jnp.float32)
    everyone = lax.all_gather(panels_here, "dp", axis=0, tiled=True).reshape(
        data_count, examples, -1
    )
    for round_at in range(rounds):
        partner = partners[round_at, data_index]
        chosen = lax.dynamic_index_in_dim(everyone, partner, 0, keepdims=False)
        score_table = place_block(score_table, score_pair(queries, chosen), data_index, round_at)
    summed = lax.psum(score_table * score_scale, ("section", "dp", "mp"))
    scores = summed.transpose(0, 2, 1, 3).reshape(data_count * asked, rounds, examples)
    return (panels_here[None], scores)


def solution(mesh):
    placed = (
        P("dp", "mp"),
        P("section", "dp", "mp"),
        P("section", "dp", "mp"),
        P("section", "mp", "dp"),
        P("section", "mp", None),
        P("section", "mp", None),
        P("section", "dp", "mp"),
        P(),
    )
    return jax.shard_map(
        body, mesh=mesh, in_specs=placed, out_specs=(P("section", "dp", "mp"), P()), check_vma=False
    )
```

profile of v0, /device:TPU:1, one launch (start us, length us, event | category | flops | bytes accessed | tf_op | source)
XLA Modules:
  0.0 635.7 jit_solution(11931362347134518088)
XLA Ops:
  25.3 87.9 %all-gather.4.cloned.1.call-done = bf16[1,1024,4096]{2,1,0:T(8,128)(2,1)} async-done(((bf16[1,1024,512]{2,1,0:T(8,128)(2,1)}), bf16[1,1024,4096]{2,1,0:T(8,128)(2,1)}) %all-gather.4.cloned.1.call-update) | async-done | bytes 8388624 | tf_op jit(solution)/shard_map/all_gather | solution.py:46
  113.8 380.4 %while.17 = (s32[]{:T(128)}, bf16[32,1024]{1,0:T(8,128)(2,1)}, bf16[128,1024]{1,0:T(8,128)(2,1)S(1)}, s32[]{:T(128)}, pred[]{:T(512)}, /*index=5*/bf16[128,1024]...) while((s32[]{:T(128)}, bf16[32,1024]{1,0:T(8,128)(2,1)}, ...), condition=%wide.region_4.5_spmd, body=%wide.region_1.4_spmd.sunk | while | flops 268959744 | bytes 9830719 | solution.py:85
  120.2 7.4 %all_gather.18 = bf16[32,4096]{1,0:T(8,128)(2,1)S(1)} all-gather(bf16[32,1024]{1,0:T(8,128)(2,1)S(1)} %get-tuple-element.282), channel_id=1, replica_groups=mesh['section'=16,'dp'=8,'mp'=4] {'mp'}, dimensions={1}, use_global_device_ids=true | all-gather | bytes 327680 | tf_op jit(solution)/shard_map/while/body/eval_jaxpr/all_gather | solution.py:62
  134.8 6.6 %all_gather.18 = bf16[32,4096]{1,0:T(8,128)(2,1)S(1)} all-gather(bf16[32,1024]{1,0:T(8,128)(2,1)S(1)} %get-tuple-element.282), channel_id=1, replica_groups=mesh['section'=16,'dp'=8,'mp'=4] {'mp'}, dimensions={1}, use_global_device_ids=true | all-gather | bytes 327680 | tf_op jit(solution)/shard_map/while/body/eval_jaxpr/all_gather | solution.py:62
  148.7 6.6 %all_gather.18 = bf16[32,4096]{1,0:T(8,128)(2,1)S(1)} all-gather(bf16[32,1024]{1,0:T(8,128)(2,1)S(1)} %get-tuple-element.282), channel_id=1, replica_groups=mesh['section'=16,'dp'=8,'mp'=4] {'mp'}, dimensions={1}, use_global_device_ids=true | all-gather | bytes 327680 | tf_op jit(solution)/shard_map/while/body/eval_jaxpr/all_gather | solution.py:62
  157.2 5.0 collective-permute-done
  163.2 6.4 %all_gather.18 = bf16[32,4096]{1,0:T(8,128)(2,1)S(1)} all-gather(bf16[32,1024]{1,0:T(8,128)(2,1)S(1)} %get-tuple-element.282), channel_id=1, replica_groups=mesh['section'=16,'dp'=8,'mp'=4] {'mp'}, dimensions={1}, use_global_device_ids=true | all-gather | bytes 327680 | tf_op jit(solution)/shard_map/while/body/eval_jaxpr/all_gather | solution.py:62
  171.5 5.8 collective-permute-done
  178.2 6.4 %all_gather.18 = bf16[32,4096]{1,0:T(8,128)(2,1)S(1)} all-gather(bf16[32,1024]{1,0:T(8,128)(2,1)S(1)} %get-tuple-element.282), channel_id=1, replica_groups=mesh['section'=16,'dp'=8,'mp'=4] {'mp'}, dimensions={1}, use_global_device_ids=true | all-gather | bytes 327680 | tf_op jit(solution)/shard_map/while/body/eval_jaxpr/all_gather | solution.py:62
  186.5 5.8 collective-permute-done
  193.2 6.4 %all_gather.18 = bf16[32,4096]{1,0:T(8,128)(2,1)S(1)} all-gather(bf16[32,1024]{1,0:T(8,128)(2,1)S(1)} %get-tuple-element.282), channel_id=1, replica_groups=mesh['section'=16,'dp'=8,'mp'=4] {'mp'}, dimensions={1}, use_global_device_ids=true | all-gather | bytes 327680 | tf_op jit(solution)/shard_map/while/body/eval_jaxpr/all_gather | solution.py:62
  201.5 5.8 collective-permute-done
  208.2 6.4 %all_gather.18 = bf16[32,4096]{1,0:T(8,128)(2,1)S(1)} all-gather(bf16[32,1024]{1,0:T(8,128)(2,1)S(1)} %get-tuple-element.282), channel_id=1, replica_groups=mesh['section'=16,'dp'=8,'mp'=4] {'mp'}, dimensions={1}, use_global_device_ids=true | all-gather | bytes 327680 | tf_op jit(solution)/shard_map/while/body/eval_jaxpr/all_gather | solution.py:62
  216.5 5.8 collective-permute-done
  223.2 6.4 %all_gather.18 = bf16[32,4096]{1,0:T(8,128)(2,1)S(1)} all-gather(bf16[32,1024]{1,0:T(8,128)(2,1)S(1)} %get-tuple-element.282), channel_id=1, replica_groups=mesh['section'=16,'dp'=8,'mp'=4] {'mp'}, dimensions={1}, use_global_device_ids=true | all-gather | bytes 327680 | tf_op jit(solution)/shard_map/while/body/eval_jaxpr/all_gather | solution.py:62
  231.5 5.8 collective-permute-done
  238.3 6.4 %all_gather.18 = bf16[32,4096]{1,0:T(8,128)(2,1)S(1)} all-gather(bf16[32,1024]{1,0:T(8,128)(2,1)S(1)} %get-tuple-element.282), channel_id=1, replica_groups=mesh['section'=16,'dp'=8,'mp'=4] {'mp'}, dimensions={1}, use_global_device_ids=true | all-gather | bytes 327680 | tf_op jit(solution)/shard_map/while/body/eval_jaxpr/all_gather | solution.py:62
  246.6 5.8 collective-permute-done
  253.3 6.4 %all_gather.18 = bf16[32,4096]{1,0:T(8,128)(2,1)S(1)} all-gather(bf16[32,1024]{1,0:T(8,128)(2,1)S(1)} %get-tuple-element.282), channel_id=1, replica_groups=mesh['section'=16,'dp'=8,'mp'=4] {'mp'}, dimensions={1}, use_global_device_ids=true | all-gather | bytes 327680 | tf_op jit(solution)/shard_map/while/body/eval_jaxpr/all_gather | solution.py:62
  261.6 8.1 %collective-permute-done = bf16[32,1024]{1,0:T(8,128)(2,1)S(1)} collective-permute-done((bf16[32,1024]{1,0:T(8,128)(2,1)}, bf16[32,1024]{1,0:T(8,128)(2,1)S(1)}, u32[]{:S(2)}, u32[]{:S(2)}) %collective-permute-start) | collective-permute-done | bytes 65568 | tf_op jit(solution)/shard_map/while/body/eval_jaxpr/ppermute | solution.py:13
  270.6 6.4 %all_gather.18 = bf16[32,4096]{1,0:T(8,128)(2,1)S(1)} all-gather(bf16[32,1024]{1,0:T(8,128)(2,1)S(1)} %get-tuple-element.282), channel_id=1, replica_groups=mesh['section'=16,'dp'=8,'mp'=4] {'mp'}, dimensions={1}, use_global_device_ids=true | all-gather | bytes 327680 | tf_op jit(solution)/shard_map/while/body/eval_jaxpr/all_gather | solution.py:62
  278.9 8.2 %collective-permute-done = bf16[32,1024]{1,0:T(8,128)(2,1)S(1)} collective-permute-done((bf16[32,1024]{1,0:T(8,128)(2,1)}, bf16[32,1024]{1,0:T(8,128)(2,1)S(1)}, u32[]{:S(2)}, u32[]{:S(2)}) %collective-permute-start) | collective-permute-done | bytes 65568 | tf_op jit(solution)/shard_map/while/body/eval_jaxpr/ppermute | solution.py:13
  288.0 6.4 %all_gather.18 = bf16[32,4096]{1,0:T(8,128)(2,1)S(1)} all-gather(bf16[32,1024]{1,0:T(8,128)(2,1)S(1)} %get-tuple-element.282), channel_id=1, replica_groups=mesh['section'=16,'dp'=8,'mp'=4] {'mp'}, dimensions={1}, use_global_device_ids=true | all-gather | bytes 327680 | tf_op jit(solution)/shard_map/while/body/eval_jaxpr/all_gather | solution.py:62
  296.3 8.2 %collective-permute-done = bf16[32,1024]{1,0:T(8,128)(2,1)S(1)} collective-permute-done((bf16[32,1024]{1,0:T(8,128)(2,1)}, bf16[32,1024]{1,0:T(8,128)(2,1)S(1)}, u32[]{:S(2)}, u32[]{:S(2)}) %collective-permute-start) | collective-permute-done | bytes 65568 | tf_op jit(solution)/shard_map/while/body/eval_jaxpr/ppermute | solution.py:13
  305.5 6.4 %all_gather.18 = bf16[32,4096]{1,0:T(8,128)(2,1)S(1)} all-gather(bf16[32,1024]{1,0:T(8,128)(2,1)S(1)} %get-tuple-element.282), channel_id=1, replica_groups=mesh['section'=16,'dp'=8,'mp'=4] {'mp'}, dimensions={1}, use_global_device_ids=true | all-gather | bytes 327680 | tf_op jit(solution)/shard_map/while/body/eval_jaxpr/all_gather | solution.py:62
  313.8 8.2 %collective-permute-done = bf16[32,1024]{1,0:T(8,128)(2,1)S(1)} collective-permute-done((bf16[32,1024]{1,0:T(8,128)(2,1)}, bf16[32,1024]{1,0:T(8,128)(2,1)S(1)}, u32[]{:S(2)}, u32[]{:S(2)}) %collective-permute-start) | collective-permute-done | bytes 65568 | tf_op jit(solution)/shard_map/while/body/eval_jaxpr/ppermute | solution.py:13
  322.9 6.4 %all_gather.18 = bf16[32,4096]{1,0:T(8,128)(2,1)S(1)} all-gather(bf16[32,1024]{1,0:T(8,128)(2,1)S(1)} %get-tuple-element.282), channel_id=1, replica_groups=mesh['section'=16,'dp'=8,'mp'=4] {'mp'}, dimensions={1}, use_global_device_ids=true | all-gather | bytes 327680 | tf_op jit(solution)/shard_map/while/body/eval_jaxpr/all_gather | solution.py:62
  331.2 8.2 %collective-permute-done = bf16[32,1024]{1,0:T(8,128)(2,1)S(1)} collective-permute-done((bf16[32,1024]{1,0:T(8,128)(2,1)}, bf16[32,1024]{1,0:T(8,128)(2,1)S(1)}, u32[]{:S(2)}, u32[]{:S(2)}) %collective-permute-start) | collective-permute-done | bytes 65568 | tf_op jit(solution)/shard_map/while/body/eval_jaxpr/ppermute | solution.py:13
  340.3 6.4 %all_gather.18 = bf16[32,4096]{1,0:T(8,128)(2,1)S(1)} all-gather(bf16[32,1024]{1,0:T(8,128)(2,1)S(1)} %get-tuple-element.282), channel_id=1, replica_groups=mesh['section'=16,'dp'=8,'mp'=4] {'mp'}, dimensions={1}, use_global_device_ids=true | all-gather | bytes 327680 | tf_op jit(solution)/shard_map/while/body/eval_jaxpr/all_gather | solution.py:62
  348.6 61.6 %collective-permute-done = bf16[32,1024]{1,0:T(8,128)(2,1)S(1)} collective-permute-done((bf16[32,1024]{1,0:T(8,128)(2,1)}, bf16[32,1024]{1,0:T(8,128)(2,1)S(1)}, u32[]{:S(2)}, u32[]{:S(2)}) %collective-permute-start) | collective-permute-done | bytes 65568 | tf_op jit(solution)/shard_map/while/body/eval_jaxpr/ppermute | solution.py:13
  411.2 6.3 all_gather.18
  417.5 6.6 %conditional.2 = (bf16[32,1024]{1,0:T(8,128)(2,1)}) conditional(s32[]{:T(128)} %convert_element_type.80, () %tuple.60, (bf16[32,1024]{1,0:T(8,128)(2,1)S(1)}, bf16[32,4096]{1,0:T(8,128)(2,1)S(1)}, bf16[1024,4096]{1,0:T(8,128)(2,1)}) %tuple.61), branch_computations={%region_2.2_spmd, %region_3.3_spmd} | conditional | flops 268533760 | bytes 8781832 | solution.py:73
  417.5 6.6 %fusion = bf16[32,1024]{1,0:T(8,128)(2,1)} fusion(bf16[32,4096]{1,0:T(8,128)(2,1)S(1)} %get-tuple-element.181, bf16[1024,4096]{1,0:T(8,128)(2,1)} %get-tuple-element.182, bf16[32,1024]{1,0:T(8,128)(2,1)S(1)} %get-tuple-element.180), kind=kOutput, calls=%fused_computation.1 | convolution fusion | flops 268533760 | bytes 8781824 | tf_op jit(solution)/shard_map/while/body/eval_jaxpr/cond/branch_1_fun/dot_general | solution.py:65
  425.4 8.2 %collective-permute-done = bf16[32,1024]{1,0:T(8,128)(2,1)S(1)} collective-permute-done((bf16[32,1024]{1,0:T(8,128)(2,1)}, bf16[32,1024]{1,0:T(8,128)(2,1)S(1)}, u32[]{:S(2)}, u32[]{:S(2)}) %collective-permute-start) | collective-permute-done | bytes 65568 | tf_op jit(solution)/shard_map/while/body/eval_jaxpr/ppermute | solution.py:13
  434.6 6.3 all_gather.18
  440.8 6.6 %conditional.2 = (bf16[32,1024]{1,0:T(8,128)(2,1)}) conditional(s32[]{:T(128)} %convert_element_type.80, () %tuple.60, (bf16[32,1024]{1,0:T(8,128)(2,1)S(1)}, bf16[32,4096]{1,0:T(8,128)(2,1)S(1)}, bf16[1024,4096]{1,0:T(8,128)(2,1)}) %tuple.61), branch_computations={%region_2.2_spmd, %region_3.3_spmd} | conditional | flops 268533760 | bytes 8781832 | solution.py:73
  440.8 6.6 %fusion = bf16[32,1024]{1,0:T(8,128)(2,1)} fusion(bf16[32,4096]{1,0:T(8,128)(2,1)S(1)} %get-tuple-element.181, bf16[1024,4096]{1,0:T(8,128)(2,1)} %get-tuple-element.182, bf16[32,1024]{1,0:T(8,128)(2,1)S(1)} %get-tuple-element.180), kind=kOutput, calls=%fused_computation.1 | convolution fusion | flops 268533760 | bytes 8781824 | tf_op jit(solution)/shard_map/while/body/eval_jaxpr/cond/branch_1_fun/dot_general | solution.py:65
  448.7 8.3 %collective-permute-done = bf16[32,1024]{1,0:T(8,128)(2,1)S(1)} collective-permute-done((bf16[32,1024]{1,0:T(8,128)(2,1)}, bf16[32,1024]{1,0:T(8,128)(2,1)S(1)}, u32[]{:S(2)}, u32[]{:S(2)}) %collective-permute-start) | collective-permute-done | bytes 65568 | tf_op jit(solution)/shard_map/while/body/eval_jaxpr/ppermute | solution.py:13
  458.0 6.3 all_gather.18
  464.3 6.6 %conditional.2 = (bf16[32,1024]{1,0:T(8,128)(2,1)}) conditional(s32[]{:T(128)} %convert_element_type.80, () %tuple.60, (bf16[32,1024]{1,0:T(8,128)(2,1)S(1)}, bf16[32,4096]{1,0:T(8,128)(2,1)S(1)}, bf16[1024,4096]{1,0:T(8,128)(2,1)}) %tuple.61), branch_computations={%region_2.2_spmd, %region_3.3_spmd} | conditional | flops 268533760 | bytes 8781832 | solution.py:73
  464.3 6.6 %fusion = bf16[32,1024]{1,0:T(8,128)(2,1)} fusion(bf16[32,4096]{1,0:T(8,128)(2,1)S(1)} %get-tuple-element.181, bf16[1024,4096]{1,0:T(8,128)(2,1)} %get-tuple-element.182, bf16[32,1024]{1,0:T(8,128)(2,1)S(1)} %get-tuple-element.180), kind=kOutput, calls=%fused_computation.1 | convolution fusion | flops 268533760 | bytes 8781824 | tf_op jit(solution)/shard_map/while/body/eval_jaxpr/cond/branch_1_fun/dot_general | solution.py:65
  472.2 8.2 %collective-permute-done = bf16[32,1024]{1,0:T(8,128)(2,1)S(1)} collective-permute-done((bf16[32,1024]{1,0:T(8,128)(2,1)}, bf16[32,1024]{1,0:T(8,128)(2,1)S(1)}, u32[]{:S(2)}, u32[]{:S(2)}) %collective-permute-start) | collective-permute-done | bytes 65568 | tf_op jit(solution)/shard_map/while/body/eval_jaxpr/ppermute | solution.py:13
  481.4 6.3 all_gather.18
  487.7 6.6 %conditional.2 = (bf16[32,1024]{1,0:T(8,128)(2,1)}) conditional(s32[]{:T(128)} %convert_element_type.80, () %tuple.60, (bf16[32,1024]{1,0:T(8,128)(2,1)S(1)}, bf16[32,4096]{1,0:T(8,128)(2,1)S(1)}, bf16[1024,4096]{1,0:T(8,128)(2,1)}) %tuple.61), branch_computations={%region_2.2_spmd, %region_3.3_spmd} | conditional | flops 268533760 | bytes 8781832 | solution.py:73
  487.7 6.6 %fusion = bf16[32,1024]{1,0:T(8,128)(2,1)} fusion(bf16[32,4096]{1,0:T(8,128)(2,1)S(1)} %get-tuple-element.181, bf16[1024,4096]{1,0:T(8,128)(2,1)} %get-tuple-element.182, bf16[32,1024]{1,0:T(8,128)(2,1)S(1)} %get-tuple-element.180), kind=kOutput, calls=%fused_computation.1 | convolution fusion | flops 268533760 | bytes 8781824 | tf_op jit(solution)/shard_map/while/body/eval_jaxpr/cond/branch_1_fun/dot_general | solution.py:65
  494.6 10.8 %all-reduce = (bf16[4,32,64]{2,1,0:T(8,128)(2,1)S(1)}, bf16[128,64]{0,1:T(8,128)(2,1)S(1)}) all-reduce(bf16[4,32,64]{2,1,0:T(8,128)(2,1)S(1)} %bitcast.104, bf16[128,64]{0,1:T(8,128)(2,1)S(1)} %convolution_convert_fusion.1), channel_id=1, replica_groups=mesh['section'=16,'dp'=8,'mp'=4] {'mp'}, use_global_device_ids=true, to_apply=%region_5.6 | all-reduce | flops 16384 | bytes 65536 | tf_op jit(solution)/shard_map/psum | solution.py:92
  505.7 18.5 %all-gather.1 = f32[8,4,1024]{2,1,0:T(4,128)S(1)} all-gather(f32[1,4,1024]{2,1,0:T(4,128)S(1)} %broadcast_in_dim_reshape.3), channel_id=1, replica_groups=mesh['section'=16,'dp'=8,'mp'=4] {'dp'}, dimensions={0}, use_global_device_ids=true | all-gather | bytes 147456 | tf_op jit(solution)/shard_map/all_gather | solution.py:108
  529.0 99.2 %psum.23 = f32[16,8,4]{1,0,2:T(8,128)S(1)} all-reduce(f32[16,8,4]{1,0,2:T(8,128)S(1)} %bitcast.105), channel_id=1, replica_groups=mesh['section'=16,'dp'=8,'mp'=4] {'section','dp','mp'}, use_global_device_ids=true, to_apply=%region_6.7 | all-reduce | flops 512 | bytes 4096 | tf_op jit(solution)/shard_map/psum | solution.py:115
  (118 shorter events, 84.2 us)
Async XLA Ops:
  7.2 17.0 %copy-start = (bf16[1,128,1024]{2,1,0:T(8,128)(2,1)S(1)}, bf16[1,128,1024]{2,1,0:T(8,128)(2,1)}, u32[]{:S(2)}) copy-start(bf16[1,128,1024]{2,1,0:T(8,128)(2,1)} %param.13) | copy-start | bytes 786436
  7.2 106.0 %all-gather.4.cloned.1.call-start = ((), (), s32[]{:S(2)}) async-start(), calls=%async_computation | async-start | bytes 9437184 | tf_op jit(solution)/shard_map/all_gather | solution.py:46
  113.8 380.5 %copy-start.2 = (bf16[1,1024,64]{1,2,0:T(8,128)(2,1)S(1)}, bf16[1,1024,64]{1,2,0:T(8,128)(2,1)}, u32[]{:S(2)}) copy-start(bf16[1,1024,64]{1,2,0:T(8,128)(2,1)} %param.17) | copy-start | bytes 393220
  113.8 410.4 %copy-start.1 = (f32[1,2,1024]{2,1,0:T(2,128)S(1)}, f32[1,2,1024]{2,1,0:T(2,128)}, u32[]{:S(2)}) copy-start(f32[1,2,1024]{2,1,0:T(2,128)} %param.18) | copy-start | bytes 24580
  113.9 5.4 collective-permute-start
  128.2 5.6 collective-permute-start
  142.1 5.6 collective-permute-start
  155.9 6.3 collective-permute-start
  170.1 7.1 %collective-permute-start = (bf16[32,1024]{1,0:T(8,128)(2,1)}, bf16[32,1024]{1,0:T(8,128)(2,1)S(1)}, u32[]{:S(2)}, u32[]{:S(2)}) collective-permute-start(bf16[32,1024]{1,0:T(8,128)(2,1)} %get-tuple-element.299), channel_id=1, source_target_pairs={{32,0},{64,32},{96,64},{128,96},{160,128},{192,160},{224,192},{256... | collective-permute-start | bytes 196616 | tf_op jit(solution)/shard_map/while/body/eval_jaxpr/ppermute | solution.py:13
  185.2 7.1 %collective-permute-start = (bf16[32,1024]{1,0:T(8,128)(2,1)}, bf16[32,1024]{1,0:T(8,128)(2,1)S(1)}, u32[]{:S(2)}, u32[]{:S(2)}) collective-permute-start(bf16[32,1024]{1,0:T(8,128)(2,1)} %get-tuple-element.299), channel_id=1, source_target_pairs={{32,0},{64,32},{96,64},{128,96},{160,128},{192,160},{224,192},{256... | collective-permute-start | bytes 196616 | tf_op jit(solution)/shard_map/while/body/eval_jaxpr/ppermute | solution.py:13
  200.2 7.1 %collective-permute-start = (bf16[32,1024]{1,0:T(8,128)(2,1)}, bf16[32,1024]{1,0:T(8,128)(2,1)S(1)}, u32[]{:S(2)}, u32[]{:S(2)}) collective-permute-start(bf16[32,1024]{1,0:T(8,128)(2,1)} %get-tuple-element.299), channel_id=1, source_target_pairs={{32,0},{64,32},{96,64},{128,96},{160,128},{192,160},{224,192},{256... | collective-permute-start | bytes 196616 | tf_op jit(solution)/shard_map/while/body/eval_jaxpr/ppermute | solution.py:13
  215.2 7.1 %collective-permute-start = (bf16[32,1024]{1,0:T(8,128)(2,1)}, bf16[32,1024]{1,0:T(8,128)(2,1)S(1)}, u32[]{:S(2)}, u32[]{:S(2)}) collective-permute-start(bf16[32,1024]{1,0:T(8,128)(2,1)} %get-tuple-element.299), channel_id=1, source_target_pairs={{32,0},{64,32},{96,64},{128,96},{160,128},{192,160},{224,192},{256... | collective-permute-start | bytes 196616 | tf_op jit(solution)/shard_map/while/body/eval_jaxpr/ppermute | solution.py:13
  230.2 7.1 %collective-permute-start = (bf16[32,1024]{1,0:T(8,128)(2,1)}, bf16[32,1024]{1,0:T(8,128)(2,1)S(1)}, u32[]{:S(2)}, u32[]{:S(2)}) collective-permute-start(bf16[32,1024]{1,0:T(8,128)(2,1)} %get-tuple-element.299), channel_id=1, source_target_pairs={{32,0},{64,32},{96,64},{128,96},{160,128},{192,160},{224,192},{256... | collective-permute-start | bytes 196616 | tf_op jit(solution)/shard_map/while/body/eval_jaxpr/ppermute | solution.py:13
  245.3 7.1 %collective-permute-start = (bf16[32,1024]{1,0:T(8,128)(2,1)}, bf16[32,1024]{1,0:T(8,128)(2,1)S(1)}, u32[]{:S(2)}, u32[]{:S(2)}) collective-permute-start(bf16[32,1024]{1,0:T(8,128)(2,1)} %get-tuple-element.299), channel_id=1, source_target_pairs={{32,0},{64,32},{96,64},{128,96},{160,128},{192,160},{224,192},{256... | collective-permute-start | bytes 196616 | tf_op jit(solution)/shard_map/while/body/eval_jaxpr/ppermute | solution.py:13
  260.3 9.4 %collective-permute-start = (bf16[32,1024]{1,0:T(8,128)(2,1)}, bf16[32,1024]{1,0:T(8,128)(2,1)S(1)}, u32[]{:S(2)}, u32[]{:S(2)}) collective-permute-start(bf16[32,1024]{1,0:T(8,128)(2,1)} %get-tuple-element.299), channel_id=1, source_target_pairs={{32,0},{64,32},{96,64},{128,96},{160,128},{192,160},{224,192},{256... | collective-permute-start | bytes 196616 | tf_op jit(solution)/shard_map/while/body/eval_jaxpr/ppermute | solution.py:13
  277.6 9.5 %collective-permute-start = (bf16[32,1024]{1,0:T(8,128)(2,1)}, bf16[32,1024]{1,0:T(8,128)(2,1)S(1)}, u32[]{:S(2)}, u32[]{:S(2)}) collective-permute-start(bf16[32,1024]{1,0:T(8,128)(2,1)} %get-tuple-element.299), channel_id=1, source_target_pairs={{32,0},{64,32},{96,64},{128,96},{160,128},{192,160},{224,192},{256... | collective-permute-start | bytes 196616 | tf_op jit(solution)/shard_map/while/body/eval_jaxpr/ppermute | solution.py:13
  295.0 9.5 %collective-permute-start = (bf16[32,1024]{1,0:T(8,128)(2,1)}, bf16[32,1024]{1,0:T(8,128)(2,1)S(1)}, u32[]{:S(2)}, u32[]{:S(2)}) collective-permute-start(bf16[32,1024]{1,0:T(8,128)(2,1)} %get-tuple-element.299), channel_id=1, source_target_pairs={{32,0},{64,32},{96,64},{128,96},{160,128},{192,160},{224,192},{256... | collective-permute-start | bytes 196616 | tf_op jit(solution)/shard_map/while/body/eval_jaxpr/ppermute | solution.py:13
  312.4 9.5 %collective-permute-start = (bf16[32,1024]{1,0:T(8,128)(2,1)}, bf16[32,1024]{1,0:T(8,128)(2,1)S(1)}, u32[]{:S(2)}, u32[]{:S(2)}) collective-permute-start(bf16[32,1024]{1,0:T(8,128)(2,1)} %get-tuple-element.299), channel_id=1, source_target_pairs={{32,0},{64,32},{96,64},{128,96},{160,128},{192,160},{224,192},{256... | collective-permute-start | bytes 196616 | tf_op jit(solution)/shard_map/while/body/eval_jaxpr/ppermute | solution.py:13
  329.9 9.5 %collective-permute-start = (bf16[32,1024]{1,0:T(8,128)(2,1)}, bf16[32,1024]{1,0:T(8,128)(2,1)S(1)}, u32[]{:S(2)}, u32[]{:S(2)}) collective-permute-start(bf16[32,1024]{1,0:T(8,128)(2,1)} %get-tuple-element.299), channel_id=1, source_target_pairs={{32,0},{64,32},{96,64},{128,96},{160,128},{192,160},{224,192},{256... | collective-permute-start | bytes 196616 | tf_op jit(solution)/shard_map/while/body/eval_jaxpr/ppermute | solution.py:13
  347.3 62.9 %collective-permute-start = (bf16[32,1024]{1,0:T(8,128)(2,1)}, bf16[32,1024]{1,0:T(8,128)(2,1)S(1)}, u32[]{:S(2)}, u32[]{:S(2)}) collective-permute-start(bf16[32,1024]{1,0:T(8,128)(2,1)} %get-tuple-element.299), channel_id=1, source_target_pairs={{32,0},{64,32},{96,64},{128,96},{160,128},{192,160},{224,192},{256... | collective-permute-start | bytes 196616 | tf_op jit(solution)/shard_map/while/body/eval_jaxpr/ppermute | solution.py:13
  424.0 9.6 %collective-permute-start = (bf16[32,1024]{1,0:T(8,128)(2,1)}, bf16[32,1024]{1,0:T(8,128)(2,1)S(1)}, u32[]{:S(2)}, u32[]{:S(2)}) collective-permute-start(bf16[32,1024]{1,0:T(8,128)(2,1)} %get-tuple-element.299), channel_id=1, source_target_pairs={{32,0},{64,32},{96,64},{128,96},{160,128},{192,160},{224,192},{256... | collective-permute-start | bytes 196616 | tf_op jit(solution)/shard_map/while/body/eval_jaxpr/ppermute | solution.py:13
  447.4 9.6 %collective-permute-start = (bf16[32,1024]{1,0:T(8,128)(2,1)}, bf16[32,1024]{1,0:T(8,128)(2,1)S(1)}, u32[]{:S(2)}, u32[]{:S(2)}) collective-permute-start(bf16[32,1024]{1,0:T(8,128)(2,1)} %get-tuple-element.299), channel_id=1, source_target_pairs={{32,0},{64,32},{96,64},{128,96},{160,128},{192,160},{224,192},{256... | collective-permute-start | bytes 196616 | tf_op jit(solution)/shard_map/while/body/eval_jaxpr/ppermute | solution.py:13
  470.9 9.6 %collective-permute-start = (bf16[32,1024]{1,0:T(8,128)(2,1)}, bf16[32,1024]{1,0:T(8,128)(2,1)S(1)}, u32[]{:S(2)}, u32[]{:S(2)}) collective-permute-start(bf16[32,1024]{1,0:T(8,128)(2,1)} %get-tuple-element.299), channel_id=1, source_target_pairs={{32,0},{64,32},{96,64},{128,96},{160,128},{192,160},{224,192},{256... | collective-permute-start | bytes 196616 | tf_op jit(solution)/shard_map/while/body/eval_jaxpr/ppermute | solution.py:13
  505.7 123.2 %copy-start.3 = (f32[1,4,1024]{2,1,0:T(4,128)}, f32[1,4,1024]{2,1,0:T(4,128)S(1)}, u32[]{:S(2)}) copy-start(f32[1,4,1024]{2,1,0:T(4,128)S(1)} %broadcast_in_dim_reshape.3) | copy-start | bytes 49156
Sparse Core Ops, SparseCore 0:
  10.1 103.0 all-gather.3
where the time goes:
time: 638 us; the launch traced here: 636 us
  waiting for transfers between devices  268 us (42%)
  blocking collectives  251 us (39%)
  matrix products  29.3 us (5%)
  between operations  28.8 us (5%)
  starting transfers between devices  24.5 us (4%)
  other arithmetic  18.2 us (3%)
  local copies, waits for them, and re-layouts  15.9 us (2%)
    ppermute x19, waiting for transfers between devices, from_behind(): return lax.ppermute(block, axis, route)  179 us
    all_gather x19, blocking collectives, advance(): grad_full = lax.all_gather(grad_piece, 'mp', axis=1, tiled=True)  122 us
    psum x1, blocking collectives, body(): summed = lax.psum(score_table * score_scale, ('section', 'dp', 'mp'))  99.2 us
    all_gather x1, waiting for transfers between devices, body(): w_rows = lax.all_gather(weights[0], 'dp', axis=1, tiled=True)  87.9 us
    dot_general x4, matrix products, through(): lax.dot_general(grad_full, w_rows, (((1,), (1,)), ((), ())), preferred_el...  26.4 us
    ppermute x19, starting transfers between devices, from_behind(): return lax.ppermute(block, axis, route)  24.5 us
    all_gather x1, blocking collectives, body(): lax.all_gather(panels_here, 'dp', axis=0, tiled=True)  18.5 us
    dynamic_update_slice x19, other arithmetic, advance(): lax.dynamic_update_slice_in_dim(stored, jnp.where(active, grad_piece, pre...  18.2 us
  transfers between devices with their start and end apart: 20, of which 20 were waited for; matrix products, arithmetic and copies ran while one was open for 0% of the time, Pallas kernels for 0%

commit v1 on v0

--- a/solution.py
+++ b/solution.py
@@ -5,6 +5,11 @@
 from jax.sharding import PartitionSpec as P
 
 LEN = 32
+
+
+def add_all(x, axis):
+    parts = lax.all_gather(x, axis)
+    return jnp.sum(parts, axis=0)
 
 
 def from_behind(block, axis, distance):
@@ -112,7 +117,7 @@
         partner = partners[round_at, data_index]
         chosen = lax.dynamic_index_in_dim(everyone, partner, 0, keepdims=False)
         score_table = place_block(score_table, score_pair(queries, chosen), data_index, round_at)
-    summed = lax.psum(score_table * score_scale, ("section", "dp", "mp"))
+    summed = add_all(score_table * score_scale, ("section", "dp", "mp"))
     scores = summed.transpose(0, 2, 1, 3).reshape(data_count * asked, rounds, examples)
     return (panels_here[None], scores)
 

time: 638 us -> 1380 us (2.16)
  waiting for transfers between devices: 268 us -> 1090 us
  blocking collectives: 251 us -> 152 us
    all_gather x0 -> x1, waiting for transfers between devices: none -> 824 us  [add_all(): parts = lax.all_gather(x, axis)]
    psum x1 -> x0, blocking collectives: 99.2 us -> none  [body(): summed = lax.psum(score_table * score_scale, ('section', 'dp', 'mp'))]
  transfers between devices with their start and end apart: 20 -> 21, of which waited for: 20 -> 21; matrix products, arithmetic and copies ran while one was open for 0% -> 0% of each run, Pallas kernels for 0% -> 0%
where the time goes in v1:
time: 1380 us; the launch traced here: 1370 us
  waiting for transfers between devices  1090 us (79%)
  blocking collectives  152 us (11%)
  matrix products  29.3 us (2%)
  other arithmetic  28.7 us (2%)
  between operations  28.6 us (2%)
  starting transfers between devices  24.5 us (2%)
  local copies, waits for them, and re-layouts  14.8 us (1%)
    all_gather x1, waiting for transfers between devices, add_all(): parts = lax.all_gather(x, axis)  824 us
    ppermute x19, waiting for transfers between devices, from_behind(): return lax.ppermute(block, axis, route)  179 us
    all_gather x19, blocking collectives, advance(): grad_full = lax.all_gather(grad_piece, 'mp', axis=1, tiled=True)  122 us
    all_gather x1, waiting for transfers between devices, body(): w_rows = lax.all_gather(weights[0], 'dp', axis=1, tiled=True)  88 us
  transfers between devices with their start and end apart: 21, of which 21 were waited for; matrix products, arithmetic and copies ran while one was open for 0% of the time, Pallas kernels for 0%

profile of v1, /device:TPU:1, one launch (start us, length us, event | category | flops | bytes accessed | tf_op | source)
XLA Modules:
  0.0 1369.8 jit_solution(1747370281964039505)
XLA Ops:
  25.2 88.0 %all-gather.6.cloned.1.call-done = bf16[1,1024,4096]{2,1,0:T(8,128)(2,1)} async-done(((bf16[1,1024,512]{2,1,0:T(8,128)(2,1)}), bf16[1,1024,4096]{2,1,0:T(8,128)(2,1)}) %all-gather.6.cloned.1.call-update) | async-done | bytes 8388624 | tf_op jit(solution)/shard_map/all_gather | solution.py:51
  113.8 380.4 %while.17 = (s32[]{:T(128)}, bf16[32,1024]{1,0:T(8,128)(2,1)}, bf16[128,1024]{1,0:T(8,128)(2,1)S(1)}, s32[]{:T(128)}, pred[]{:T(512)}, /*index=5*/bf16[128,1024]...) while((s32[]{:T(128)}, bf16[32,1024]{1,0:T(8,128)(2,1)}, ...), condition=%wide.region_4.5_spmd, body=%wide.region_1.4_spmd.sunk | while | flops 268959744 | bytes 9830719 | solution.py:90
  120.2 7.4 all_gather.26
  134.8 6.6 all_gather.26
  148.6 6.6 all_gather.26
  163.1 6.4 all_gather.26
  171.4 5.8 collective-permute-done
  178.2 6.4 all_gather.26
  186.5 5.8 collective-permute-done
  193.2 6.4 all_gather.26
  201.5 5.8 collective-permute-done
  208.2 6.4 all_gather.26
  216.5 5.8 collective-permute-done
  223.2 6.4 all_gather.26
  231.5 5.8 collective-permute-done
  238.2 6.4 all_gather.26
  246.5 5.8 collective-permute-done
  253.3 6.4 all_gather.26
  261.6 8.0 collective-permute-done
  270.6 6.4 all_gather.26
  278.9 8.2 collective-permute-done
  288.0 6.4 all_gather.26
  296.3 8.2 collective-permute-done
  305.4 6.4 all_gather.26
  313.7 8.2 collective-permute-done
  322.8 6.4 all_gather.26
  331.1 8.2 collective-permute-done
  340.2 6.4 all_gather.26
  348.5 61.6 %collective-permute-done = bf16[32,1024]{1,0:T(8,128)(2,1)S(1)} collective-permute-done((bf16[32,1024]{1,0:T(8,128)(2,1)}, bf16[32,1024]{1,0:T(8,128)(2,1)S(1)}, u32[]{:S(2)}, u32[]{:S(2)}) %collective-permute-start) | collective-permute-done | bytes 65568 | tf_op jit(solution)/shard_map/while/body/eval_jaxpr/ppermute | solution.py:18
  411.1 6.4 all_gather.26
  417.4 6.6 conditional.2
  417.4 6.6 fusion
  425.3 8.2 collective-permute-done
  434.5 6.4 all_gather.26
  440.8 6.6 conditional.2
  440.8 6.6 fusion
  448.7 8.2 collective-permute-done
  457.9 6.4 all_gather.26
  464.3 6.6 conditional.2
  464.3 6.6 fusion
  472.2 8.2 collective-permute-done
  481.3 6.4 all_gather.26
  487.7 6.6 conditional.2
  487.7 6.6 fusion
  494.6 10.8 all-reduce
  505.7 18.6 %all-gather.2 = f32[8,4,1024]{2,1,0:T(4,128)S(1)} all-gather(f32[1,4,1024]{2,1,0:T(4,128)S(1)} %broadcast_in_dim_reshape.3), channel_id=1, replica_groups=mesh['section'=16,'dp'=8,'mp'=4] {'dp'}, dimensions={0}, use_global_device_ids=true | all-gather | bytes 147456 | tf_op jit(solution)/shard_map/all_gather | solution.py:113
  528.6 823.8 %all-gather.8.cloned.1.call-done = f32[4096,8,2,4]{1,3,2,0:T(4,128)} async-done(((f32[8,8,2,4]{1,3,2,0:T(4,128)}), f32[4096,8,2,4]{1,3,2,0:T(4,128)}) %all-gather.8.cloned.1.call-update) | async-done | bytes 1048592 | tf_op jit(solution)/shard_map/all_gather | solution.py:11
  1352.4 9.9 reduce_sum.9
  (122 shorter events, 88.7 us)
Async XLA Ops:
  7.2 16.9 %copy-start = (bf16[1,128,1024]{2,1,0:T(8,128)(2,1)S(1)}, bf16[1,128,1024]{2,1,0:T(8,128)(2,1)}, u32[]{:S(2)}) copy-start(bf16[1,128,1024]{2,1,0:T(8,128)(2,1)} %param.13) | copy-start | bytes 786436
  7.2 106.0 %all-gather.6.cloned.1.call-start = ((), (), s32[]{:S(2)}) async-start(), calls=%async_computation | async-start | bytes 9437184 | tf_op jit(solution)/shard_map/all_gather | solution.py:51
  7.9 1344.5 %all-gather.8.cloned.1.call-start = ((), (), s32[]{:S(2)}) async-start(), calls=%async_computation.1 | async-start | bytes 16809984 | tf_op jit(solution)/shard_map/all_gather | solution.py:11
  113.8 380.4 %copy-start.2 = (bf16[1,1024,64]{1,2,0:T(8,128)(2,1)S(1)}, bf16[1,1024,64]{1,2,0:T(8,128)(2,1)}, u32[]{:S(2)}) copy-start(bf16[1,1024,64]{1,2,0:T(8,128)(2,1)} %param.17) | copy-start | bytes 393220
  113.8 410.4 %copy-start.1 = (f32[1,2,1024]{2,1,0:T(2,128)S(1)}, f32[1,2,1024]{2,1,0:T(2,128)}, u32[]{:S(2)}) copy-start(f32[1,2,1024]{2,1,0:T(2,128)} %param.18) | copy-start | bytes 24580
  113.9 5.4 collective-permute-start
  128.2 5.6 collective-permute-start
  142.0 5.6 collective-permute-start
  155.9 6.3 collective-permute-start
  170.1 7.1 collective-permute-start
  185.2 7.1 collective-permute-start
  200.2 7.1 collective-permute-start
  215.2 7.1 collective-permute-start
  230.2 7.1 collective-permute-start
  245.2 7.1 collective-permute-start
  260.2 9.4 collective-permute-start
  277.5 9.5 collective-permute-start
  295.0 9.5 collective-permute-start
  312.4 9.5 collective-permute-start
  329.8 9.5 collective-permute-start
  347.2 62.9 %collective-permute-start = (bf16[32,1024]{1,0:T(8,128)(2,1)}, bf16[32,1024]{1,0:T(8,128)(2,1)S(1)}, u32[]{:S(2)}, u32[]{:S(2)}) collective-permute-start(bf16[32,1024]{1,0:T(8,128)(2,1)} %get-tuple-element.299), channel_id=1, source_target_pairs={{32,0},{64,32},{96,64},{128,96},{160,128},{192,160},{224,192},{256... | collective-permute-start | bytes 196616 | tf_op jit(solution)/shard_map/while/body/eval_jaxpr/ppermute | solution.py:18
  424.0 9.5 collective-permute-start
  447.4 9.5 collective-permute-start
  470.9 9.5 collective-permute-start
  505.7 856.6 %copy-start.3 = (f32[1,4,1024]{2,1,0:T(4,128)}, f32[1,4,1024]{2,1,0:T(4,128)S(1)}, u32[]{:S(2)}) copy-start(f32[1,4,1024]{2,1,0:T(4,128)S(1)} %broadcast_in_dim_reshape.3) | copy-start | bytes 49156
Sparse Core Ops, SparseCore 0:
  10.1 103.0 all-gather.5
  528.7 823.6 all-gather.7
